TPU v7x, 256 devices: a whole 4x4x8 slice. The times are simulated.
256 devices in a mesh: section: 4 (over x_hi, core), expert: 4 (over y), dp: 16 (over z, x_lo).
Axes of the slice: x: 4 (x_hi: 2, x_lo: 2; x = x_hi * 2 + x_lo), y: 4, z: 8, core: 2. Of those that a mesh axis runs over, the one named last changes fastest.
Arguments:
- tokens: bfloat16 [2, 4096, 3072], P(None, ('expert', 'dp')), may hold values from -6 to 6
- routes: int32 [2, 4096, 2], P(None, ('expert', 'dp')), may hold values from 0 to 3, all different within a row; in each aligned block of 64 rows (0 to 63, 64 to 127, ..., all dimensions but the last counted through in order) at most 36 rows name the same one
- router: bfloat16 [3072, 4], replicated, may hold values from -0.109375 to 0.109375
- gate_weight: bfloat16 [4, 8192, 3072], P('expert', ('section', 'dp')), may hold values from -0.109375 to 0.109375
- up_weight: bfloat16 [4, 8192, 3072], P('expert', ('section', 'dp')), may hold values from -0.109375 to 0.109375
- down_weight: bfloat16 [4, 8192, 3072], P('expert', ('section', 'dp')), may hold values from -0.0625 to 0.0625
Outputs:
- activations: bfloat16 [2, 4096, 3072], P(None, ('expert', 'dp'), 'section')
- gram: bfloat16 [4, 3072, 3072], P('expert', ('section', 'dp'))
Inputs may be any that keep to these rules, and one draw needn't show every extreme that they name: `routes`: in every micro-batch, each aligned block of 64 tokens (the tokens of one device) names no expert more than 36 times, a bound that some block reaches; the two experts of a token differ; every expert is named somewhere.
All inputs are finite; a program needn't handle non-finite values.
Results may differ from a plain program's by a relative error of at most 0.02.
Values may be sent and summed in bfloat16 or wider, within the bound.
No kernel may reach another device: no remote copies, remote signals or barrier semaphores. Data moves between devices by JAX's collectives and lax.ppermute only.
A program may use at most 128 MiB of HBM per device.

v0:
```python
import jax
import jax.numpy as jnp
from jax import lax
from jax.sharding import PartitionSpec as P


def route_targets(route_ids, experts, capacity):
    onehot = (route_ids[:, :, None] == jnp.arange(experts, dtype=jnp.int32)[None, None, :]).astype(
        jnp.int32
    )
    flattened = onehot.reshape(-1, experts)
    before = jnp.cumsum(flattened, axis=0) - flattened
    slot_rank = jnp.sum(before * flattened, axis=1).reshape(route_ids.shape)
    return route_ids * capacity + slot_rank


def on_device(tokens, routes, router, gate_weight, up_weight, down_weight):
    micro_count = tokens.shape[0]
    rows_dev = tokens.shape[1]
    model_width = tokens.shape[2]
    experts = router.shape[1]
    capacity = 9 * rows_dev // (4 * experts)
    section_count = lax.axis_size("section")
    replicas = lax.axis_size("dp")
    section_index = lax.axis_index("section")
    col_width = model_width // section_count
    gate_rows = gate_weight[0]
    up_rows = up_weight[0]
    down_rows = down_weight[0]
    logits = jnp.einsum("mtd,de->mte", tokens, router, preferred_element_type=jnp.float32)
    chosen = jnp.take_along_axis(logits, routes, axis=-1)
    logit_gap = chosen[..., 0] - chosen[..., 1]
    first_gate = jax.nn.sigmoid(logit_gap)
    second_gate = jax.nn.sigmoid(-logit_gap)
    target = jax.vmap(lambda one_block: route_targets(one_block, experts, capacity))(routes)
    slot_ids = jnp.arange(experts * capacity, dtype=jnp.int32)
    placing = jnp.sum(
        (slot_ids[None, :, None, None] == target[:, None, :, :]).astype(jnp.float32), axis=3
    ).astype(jnp.bfloat16)
    outgoing = jnp.einsum(
        "mst,mtd->msd", placing, tokens, preferred_element_type=jnp.float32
    ).astype(jnp.bfloat16)
    outgoing = outgoing.reshape(micro_count, experts, capacity, model_width)
    arrived = lax.all_to_all(outgoing, "expert", split_axis=1, concat_axis=1, tiled=True)
    rows_all = arrived.reshape(-1, model_width)
    gate_piece = lax.all_gather(gate_rows, "dp", axis=0, tiled=True)
    up_piece = lax.all_gather(up_rows, "dp", axis=0, tiled=True)
    down_piece = lax.all_gather(down_rows, "dp", axis=0, tiled=True)
    gate_part = lax.dot_general(
        rows_all, gate_piece, (((1,), (1,)), ((), ())), preferred_element_type=jnp.float32
    )
    up_part = lax.dot_general(
        rows_all, up_piece, (((1,), (1,)), ((), ())), preferred_element_type=jnp.float32
    )
    inner_units = (jax.nn.silu(gate_part) * up_part).astype(jnp.bfloat16)
    partial_out = jnp.dot(inner_units, down_piece, preferred_element_type=jnp.float32)
    summed_out = lax.psum_scatter(
        partial_out.astype(jnp.bfloat16), "section", scatter_dimension=1, tiled=True
    )
    expert_out = summed_out.reshape(micro_count, experts, capacity, col_width)
    returned = lax.all_to_all(expert_out, "expert", split_axis=1, concat_axis=1, tiled=True)
    flat_back = returned.reshape(micro_count, experts * capacity, col_width)
    first_rows = jnp.take_along_axis(flat_back, target[:, :, 0][:, :, None], axis=1).astype(
        jnp.float32
    )
    second_rows = jnp.take_along_axis(flat_back, target[:, :, 1][:, :, None], axis=1).astype(
        jnp.float32
    )
    own_cols = lax.dynamic_slice_in_dim(tokens, section_index * col_width, col_width, 2).astype(
        jnp.float32
    )
    layer_out = (
        own_cols + first_gate[..., None] * first_rows + second_gate[..., None] * second_rows
    ).astype(jnp.bfloat16)
    all_tokens = rows_dev * lax.axis_size("expert") * replicas
    gram_scale = experts / (2.0 * micro_count * all_tokens)
    block_rows = col_width // replicas
    left_cols = lax.dynamic_slice_in_dim(
        rows_all, section_index * col_width, block_rows * lax.axis_size("dp"), 1
    )
    product = (
        lax.dot_general(
            left_cols, rows_all, (((0,), (0,)), ((), ())), preferred_element_type=jnp.float32
        )
        * gram_scale
    )
    rounded = lax.optimization_barrier(product.astype(jnp.bfloat16))
    gram_block = lax.psum_scatter(
        rounded.astype(jnp.float32).astype(jnp.bfloat16), "dp", scatter_dimension=0, tiled=True
    )
    return (layer_out, gram_block[None])


def solution(mesh):
    return jax.shard_map(
        on_device,
        mesh=mesh,
        in_specs=(
            P(None, ("expert", "dp"), None),
            P(None, ("expert", "dp"), None),
            P(),
            P("expert", ("section", "dp"), None),
            P("expert", ("section", "dp"), None),
            P("expert", ("section", "dp"), None),
        ),
        out_specs=(P(None, ("expert", "dp"), "section"), P("expert", ("section", "dp"), None)),
        check_vma=False,
    )
```

profile of v0, /device:TPU:50, one launch (start us, length us, event | category | flops | bytes accessed | tf_op | source)
XLA Modules:
  0.0 997.7 jit_solution(10317960741379310035)
XLA Ops:
  7.2 0.7 all-gather.7.cloned.1.call-update
  8.0 0.7 all-gather.11.cloned.1.call-update
  8.7 0.7 all-gather.9.cloned.1.call-update
  9.6 0.1 eq.30
  9.8 0.2 reduce_window_sum.11
  10.0 0.2 select_reduce_fusion
  10.2 0.1 reshape.35
  10.6 0.7 convolution_convert_fusion
  11.2 1.8 copy.70
  13.1 24.9 %all_to_all.10 = bf16[2,4,36,3072]{3,0,2,1:T(2,128)(2,1)S(1)} all-to-all(bf16[2,4,36,3072]{3,0,2,1:T(2,128)(2,1)S(1)} %bitcast.45), channel_id=1, replica_groups=mesh['section'=4,'expert'=4,'dp'=16] {'expert'}, dimensions={1} | all-to-all | bytes 3538944 | tf_op jit(solution)/shard_map/all_to_all | solution.py:44
  38.0 0.4 copy.71
  38.4 1.4 reshape.37
  39.8 243.2 %all-gather.7.cloned.1.call-done = bf16[1,2048,3072]{2,1,0:T(8,128)(2,1)} async-done(((bf16[1,128,3072]{2,1,0:T(8,128)(2,1)}), bf16[1,2048,3072]{2,1,0:T(8,128)(2,1)}) %all-gather.7.cloned.1.call-update) | async-done | bytes 12582928 | tf_op jit(solution)/shard_map/all_gather | solution.py:46
  283.0 10.4 %fusion.4 = f32[288,2048]{1,0:T(8,128)} fusion(bf16[288,3072]{1,0:T(8,128)(2,1)} %reshape.37, bf16[1,2048,3072]{2,1,0:T(8,128)(2,1)} %all-gather.7.cloned.1.call-done), kind=kOutput, calls=%fused_computation.7 | convolution fusion | flops 3623878656 | bytes 16711680 | tf_op jit(solution)/shard_map/dot_general | solution.py:49
  293.4 260.4 %all-gather.11.cloned.1.call-done = bf16[1,2048,3072]{2,1,0:T(8,128)(2,1)} async-done(((bf16[1,128,3072]{2,1,0:T(8,128)(2,1)}), bf16[1,2048,3072]{2,1,0:T(8,128)(2,1)}) %all-gather.11.cloned.1.call-update) | async-done | bytes 12582928 | tf_op jit(solution)/shard_map/all_gather | solution.py:48
  553.7 270.7 %all-gather.9.cloned.1.call-done = bf16[1,2048,3072]{2,1,0:T(8,128)(2,1)} async-done(((bf16[1,128,3072]{2,1,0:T(8,128)(2,1)}), bf16[1,2048,3072]{2,1,0:T(8,128)(2,1)}) %all-gather.9.cloned.1.call-update) | async-done | bytes 12582928 | tf_op jit(solution)/shard_map/all_gather | solution.py:47
  824.5 14.5 %fusion.6 = bf16[288,3072]{1,0:T(8,128)(2,1)} fusion(bf16[1,2048,3072]{2,1,0:T(8,128)(2,1)} %all-gather.11.cloned.1.call-done, bf16[288,3072]{1,0:T(8,128)(2,1)S(1)} %copy-done.2, bf16[1,2048,3072]{2,1,0:T(8,128)(2,1)} %all-gather.9.cloned.1.call-done, f32[288,2048]{1,0:T(8,128)} %fusion.4), kind=kOutput, calls=%fused_computation.11 | convolution fusion | flops 7252180992 | bytes 31064064 | tf_op jit(solution)/shard_map/dot_general | solution.py:56
  839.0 0.2 reduce-scatter.5.cloned.1.call-start
  839.3 4.4 multiply_convert_fusion
  843.8 0.1 reshape.52
  844.0 0.4 fusion.20
  844.4 2.8 gather_fusion
  847.2 0.1 reshape.55
  847.4 30.2 %reduce-scatter.3.cloned.1.call-done = bf16[288,768]{1,0:T(8,128)(2,1)} async-done(((bf16[288,3072]{1,0:T(8,128)(2,1)}), bf16[288,768]{1,0:T(8,128)(2,1)}) %reduce-scatter.3.cloned.1.call-update) | async-done | bytes 442384 | tf_op jit(solution)/shard_map/reduce_scatter | solution.py:57
  877.6 1.1 reshape.38
  878.7 1.2 copy.72
  879.9 4.8 all-to-all-start.1
  884.9 5.3 all-to-all-done.1
  890.3 1.5 gather_fusion.1
  891.8 1.5 gather_fusion.2
  893.3 0.9 add_convert_fusion
  894.2 97.1 %reduce-scatter.5.cloned.1.call-done = bf16[48,3072]{1,0:T(8,128)(2,1)} async-done(((bf16[768,3072]{1,0:T(8,128)(2,1)}), bf16[48,3072]{1,0:T(8,128)(2,1)}) %reduce-scatter.5.cloned.1.call-update) | async-done | bytes 294928 | tf_op jit(solution)/shard_map/reduce_scatter | solution.py:88
  (30 shorter events, 1.1 us)
Async XLA Ops:
  7.2 836.8 %copy-start = (bf16[3072,4]{0,1:T(4,128)(2,1)S(1)}, bf16[3072,4]{0,1:T(4,128)(2,1)}, u32[]{:S(2)}) copy-start(bf16[3072,4]{0,1:T(4,128)(2,1)} %param.10) | copy-start | bytes 73732
  7.2 2.3 copy-start.3
  7.2 3.4 copy-start.1
  7.2 275.8 %all-gather.7.cloned.1.call-start = ((), (), s32[]{:S(2)}) async-start(), calls=%async_computation.6 | async-start | bytes 13369344 | tf_op jit(solution)/shard_map/all_gather | solution.py:46
  7.9 545.8 %all-gather.11.cloned.1.call-start = ((), (), s32[]{:S(2)}) async-start(), calls=%async_computation.8 | async-start | bytes 13369344 | tf_op jit(solution)/shard_map/all_gather | solution.py:48
  8.7 815.8 %all-gather.9.cloned.1.call-start = ((), (), s32[]{:S(2)}) async-start(), calls=%async_computation.7 | async-start | bytes 13369344 | tf_op jit(solution)/shard_map/all_gather | solution.py:47
  9.4 868.2 %reduce-scatter.3.cloned.1.call-start = ((), (), s32[]{:S(2)}) async-start(), calls=%async_computation.4 | async-start | bytes 2211840 | tf_op jit(solution)/shard_map/reduce_scatter | solution.py:57
  39.8 784.7 %copy-start.2 = (bf16[288,3072]{1,0:T(8,128)(2,1)S(1)}, bf16[288,3072]{1,0:T(8,128)(2,1)}, u32[]{:S(2)}) copy-start(bf16[288,3072]{1,0:T(8,128)(2,1)} %reshape.37) | copy-start | bytes 5308420
  839.0 152.2 %reduce-scatter.5.cloned.1.call-start = ((), (), s32[]{:S(2)}) async-start(), calls=%async_computation.5 | async-start | bytes 5013504 | tf_op jit(solution)/shard_map/reduce_scatter | solution.py:88
  879.9 10.3 %all-to-all-start.1 = ((bf16[2,4,36,768]{3,0,2,1:T(2,128)(2,1)}), bf16[2,4,36,768]{3,0,2,1:T(2,128)(2,1)S(1)}, u32[]{:S(2)}, u32[]{:S(2)}) async-start(bf16[2,4,36,768]{3,0,2,1:T(2,128)(2,1)} %copy.72), calls=%async_computation.2 | async-start | bytes 884736 | tf_op jit(solution)/shard_map/all_to_all | solution.py:61
Sparse Core Ops, SparseCore 0:
  9.8 273.1 all-gather.6
  284.8 268.8 all-gather.10
  555.5 268.8 all-gather.8
  839.1 38.4 reduce-scatter.2
  880.6 110.5 reduce-scatter.4
where the time goes:
time: 998 us
  waiting for transfers between devices  909 us (91%)
  matrix products  30.4 us (3%)
  blocking collectives  24.9 us (2%)
  between operations  14 us (1%)
  local copies, waits for them, and re-layouts  12.9 us (1%)
    all_gather x1, waiting for transfers between devices, on_device(): up_piece = lax.all_gather(up_rows, 'dp', axis=0, tiled=True)  271 us
    all_gather x1, waiting for transfers between devices, on_device(): down_piece = lax.all_gather(down_rows, 'dp', axis=0, tiled=True)  260 us
    all_gather x1, waiting for transfers between devices, on_device(): gate_piece = lax.all_gather(gate_rows, 'dp', axis=0, tiled=True)  243 us
    reduce_scatter x1, waiting for transfers between devices, on_device(): lax.psum_scatter(rounded.astype(jnp.float32).astype(jnp.bfloat16), 'dp',...  97.1 us
    reduce_scatter x1, waiting for transfers between devices, on_device(): lax.psum_scatter(partial_out.astype(jnp.bfloat16), 'section', scatter_dim...  30.2 us
    all_to_all x1, blocking collectives, on_device(): lax.all_to_all(outgoing, 'expert', split_axis=1, concat_axis=1, tiled=True)  24.9 us
  transfers between devices with their start and end apart: 6, of which 6 were waited for; matrix products, arithmetic and copies ran while one was open for 3% of the time, Pallas kernels for 0%

commit v1 on v0

--- a/solution.py
+++ b/solution.py
@@ -41,7 +41,12 @@
         "mst,mtd->msd", placing, tokens, preferred_element_type=jnp.float32
     ).astype(jnp.bfloat16)
     outgoing = outgoing.reshape(micro_count, experts, capacity, model_width)
-    arrived = lax.all_to_all(outgoing, "expert", split_axis=1, concat_axis=1, tiled=True)
+    arrived = jnp.concatenate(
+        lax.all_to_all(
+            jnp.stack(jnp.split(outgoing, lax.axis_size("expert"), axis=1)), "expert", 0, 0
+        ),
+        axis=1,
+    )
     rows_all = arrived.reshape(-1, model_width)
     gate_piece = lax.all_gather(gate_rows, "dp", axis=0, tiled=True)
     up_piece = lax.all_gather(up_rows, "dp", axis=0, tiled=True)

time: 998 us -> 1000 us (level)
  no operation moved by 1% of the time
where the time goes in v1:
time: 1000 us; the launch traced here: 999 us
  waiting for transfers between devices  906 us (91%)
  matrix products  30.3 us (3%)
  blocking collectives  24.9 us (2%)
  local copies, waits for them, and re-layouts  14.1 us (1%)
  between operations  14 us (1%)
    all_gather x1, waiting for transfers between devices, on_device(): up_piece = lax.all_gather(up_rows, 'dp', axis=0, tiled=True)  271 us
    all_gather x1, waiting for transfers between devices, on_device(): down_piece = lax.all_gather(down_rows, 'dp', axis=0, tiled=True)  262 us
    all_gather x1, waiting for transfers between devices, on_device(): gate_piece = lax.all_gather(gate_rows, 'dp', axis=0, tiled=True)  239 us
    reduce_scatter x1, waiting for transfers between devices, on_device(): lax.psum_scatter(rounded.astype(jnp.float32).astype(jnp.bfloat16), 'dp',...  96.9 us
    reduce_scatter x1, waiting for transfers between devices, on_device(): lax.psum_scatter(partial_out.astype(jnp.bfloat16), 'section', scatter_dim...  30.5 us
    all_to_all x1, blocking collectives, on_device(): lax.all_to_all(jnp.stack(jnp.split(outgoing, lax.axis_size('expert'), axi...  24.9 us
  transfers between devices with their start and end apart: 6, of which 6 were waited for; matrix products, arithmetic and copies ran while one was open for 3% of the time, Pallas kernels for 0%

profile of v1, /device:TPU:50, one launch (start us, length us, event | category | flops | bytes accessed | tf_op | source)
XLA Modules:
  0.0 999.5 jit_solution(87970168178617235)
XLA Ops:
  7.2 0.7 all-gather.7.cloned.1.call-update
  8.0 0.7 all-gather.11.cloned.1.call-update
  8.7 0.7 all-gather.9.cloned.1.call-update
  9.6 0.1 eq.30
  9.8 0.2 reduce_window_sum.11
  10.0 0.2 select_reduce_fusion
  10.2 0.1 reshape.35
  10.6 0.7 convolution_convert_fusion
  11.2 1.8 copy.73
  13.1 1.2 slice_bitcast_fusion.3
  14.3 3.3 pad_maximum_fusion
  17.6 24.9 %all_to_all.10 = bf16[4,2,1,36,3072]{4,1,3,2,0:T(2,128)(2,1)S(1)} all-to-all(bf16[4,2,1,36,3072]{4,1,3,2,0:T(2,128)(2,1)S(1)} %pad_maximum_fusion), channel_id=1, replica_groups=mesh['section'=4,'expert'=4,'dp'=16] {'expert'}, dimensions={0} | all-to-all | bytes 3538944 | tf_op jit(solution)/shard_map/all_to_all | solution.py:45
  42.5 0.4 copy.74
  42.9 1.4 reshape_reshape.3
  44.3 238.7 %all-gather.7.cloned.1.call-done = bf16[1,2048,3072]{2,1,0:T(8,128)(2,1)} async-done(((bf16[1,128,3072]{2,1,0:T(8,128)(2,1)}), bf16[1,2048,3072]{2,1,0:T(8,128)(2,1)}) %all-gather.7.cloned.1.call-update) | async-done | bytes 12582928 | tf_op jit(solution)/shard_map/all_gather | solution.py:51
  283.0 10.4 %fusion.4 = f32[288,2048]{1,0:T(8,128)} fusion(bf16[288,3072]{1,0:T(8,128)(2,1)} %reshape_reshape.3, bf16[1,2048,3072]{2,1,0:T(8,128)(2,1)} %all-gather.7.cloned.1.call-done), kind=kOutput, calls=%fused_computation.7 | convolution fusion | flops 3623878656 | bytes 16711680 | tf_op jit(solution)/shard_map/dot_general | solution.py:54
  293.4 262.2 %all-gather.11.cloned.1.call-done = bf16[1,2048,3072]{2,1,0:T(8,128)(2,1)} async-done(((bf16[1,128,3072]{2,1,0:T(8,128)(2,1)}), bf16[1,2048,3072]{2,1,0:T(8,128)(2,1)}) %all-gather.11.cloned.1.call-update) | async-done | bytes 12582928 | tf_op jit(solution)/shard_map/all_gather | solution.py:53
  555.6 270.7 %all-gather.9.cloned.1.call-done = bf16[1,2048,3072]{2,1,0:T(8,128)(2,1)} async-done(((bf16[1,128,3072]{2,1,0:T(8,128)(2,1)}), bf16[1,2048,3072]{2,1,0:T(8,128)(2,1)}) %all-gather.9.cloned.1.call-update) | async-done | bytes 12582928 | tf_op jit(solution)/shard_map/all_gather | solution.py:52
  826.3 14.5 %fusion.6 = bf16[288,3072]{1,0:T(8,128)(2,1)} fusion(bf16[1,2048,3072]{2,1,0:T(8,128)(2,1)} %all-gather.11.cloned.1.call-done, bf16[288,3072]{1,0:T(8,128)(2,1)S(1)} %copy-done.2, bf16[1,2048,3072]{2,1,0:T(8,128)(2,1)} %all-gather.9.cloned.1.call-done, f32[288,2048]{1,0:T(8,128)} %fusion.4), kind=kOutput, calls=%fused_computation.11 | convolution fusion | flops 7252180992 | bytes 31064064 | tf_op jit(solution)/shard_map/dot_general | solution.py:61
  840.9 4.4 multiply_convert_fusion
  845.4 0.1 reshape.52
  845.6 0.4 fusion.20
  846.0 2.8 gather_fusion
  849.1 30.5 %reduce-scatter.3.cloned.1.call-done = bf16[288,768]{1,0:T(8,128)(2,1)} async-done(((bf16[288,3072]{1,0:T(8,128)(2,1)}), bf16[288,768]{1,0:T(8,128)(2,1)}) %reduce-scatter.3.cloned.1.call-update) | async-done | bytes 442384 | tf_op jit(solution)/shard_map/reduce_scatter | solution.py:62
  879.5 1.1 reshape.38
  880.6 1.2 copy.75
  881.9 4.8 all-to-all-start.1
  886.9 5.3 all-to-all-done.1
  892.2 1.5 gather_fusion.1
  893.7 1.5 gather_fusion.2
  895.2 0.9 add_convert_fusion
  896.0 96.9 %reduce-scatter.5.cloned.1.call-done = bf16[48,3072]{1,0:T(8,128)(2,1)} async-done(((bf16[768,3072]{1,0:T(8,128)(2,1)}), bf16[48,3072]{1,0:T(8,128)(2,1)}) %reduce-scatter.5.cloned.1.call-update) | async-done | bytes 294928 | tf_op jit(solution)/shard_map/reduce_scatter | solution.py:93
  (32 shorter events, 1.2 us)
Async XLA Ops:
  7.2 838.4 %copy-start = (bf16[3072,4]{0,1:T(4,128)(2,1)S(1)}, bf16[3072,4]{0,1:T(4,128)(2,1)}, u32[]{:S(2)}) copy-start(bf16[3072,4]{0,1:T(4,128)(2,1)} %param.10) | copy-start | bytes 73732
  7.2 2.3 copy-start.3
  7.2 3.4 copy-start.1
  7.2 275.8 %all-gather.7.cloned.1.call-start = ((), (), s32[]{:S(2)}) async-start(), calls=%async_computation.6 | async-start | bytes 13369344 | tf_op jit(solution)/shard_map/all_gather | solution.py:51
  7.9 547.6 %all-gather.11.cloned.1.call-start = ((), (), s32[]{:S(2)}) async-start(), calls=%async_computation.8 | async-start | bytes 13369344 | tf_op jit(solution)/shard_map/all_gather | solution.py:53
  8.7 817.6 %all-gather.9.cloned.1.call-start = ((), (), s32[]{:S(2)}) async-start(), calls=%async_computation.7 | async-start | bytes 13369344 | tf_op jit(solution)/shard_map/all_gather | solution.py:52
  9.4 870.1 %reduce-scatter.3.cloned.1.call-start = ((), (), s32[]{:S(2)}) async-start(), calls=%async_computation.4 | async-start | bytes 2211840 | tf_op jit(solution)/shard_map/reduce_scatter | solution.py:62
  44.3 781.9 %copy-start.2 = (bf16[288,3072]{1,0:T(8,128)(2,1)S(1)}, bf16[288,3072]{1,0:T(8,128)(2,1)}, u32[]{:S(2)}) copy-start(bf16[288,3072]{1,0:T(8,128)(2,1)} %reshape_reshape.3) | copy-start | bytes 5308420
  840.9 152.1 %reduce-scatter.5.cloned.1.call-start = ((), (), s32[]{:S(2)}) async-start(), calls=%async_computation.5 | async-start | bytes 5013504 | tf_op jit(solution)/shard_map/reduce_scatter | solution.py:93
  881.9 10.3 %all-to-all-start.1 = ((bf16[2,4,36,768]{3,0,2,1:T(2,128)(2,1)}), bf16[2,4,36,768]{3,0,2,1:T(2,128)(2,1)S(1)}, u32[]{:S(2)}, u32[]{:S(2)}) async-start(bf16[2,4,36,768]{3,0,2,1:T(2,128)(2,1)} %copy.75), calls=%async_computation.2 | async-start | bytes 884736 | tf_op jit(solution)/shard_map/all_to_all | solution.py:66
Sparse Core Ops, SparseCore 0:
  9.8 273.1 all-gather.6
  284.8 270.7 all-gather.10
  557.4 268.8 all-gather.8
  841.0 38.4 reduce-scatter.2
  882.5 110.3 reduce-scatter.4
